TPU v7x, 32 devices: a whole 2x2x4 slice. The times are simulated.
32 devices in a mesh: sample: 16 (over z, x, core), block: 2 (over y).
Axes of the slice: x: 2, y: 2, z: 4, core: 2. Of those that a mesh axis runs over, the one named last changes fastest.
Arguments:
- genotype: int32 [16384, 2000], P('sample', 'block'), may hold values from 0 to 2
- allele_freq: float32 [2000], P('block'), may hold values from 0.05 to 0.5
- phenotype: bfloat16 [16384, 16], P('sample'), may hold values from -6 to 6
- shrinkage: float32 [2], replicated, may hold values from 0.05 to 2
- owner_order: int32 [16], replicated, may hold values from 0 to 15, each once
Outputs:
- predictions: bfloat16 [16, 8, 16384], P('block', None, 'sample')
Inputs may be any that keep to these rules, and one draw needn't show every extreme that they name: `owner_order`: each phenotype appears once.
All inputs are finite; a program needn't handle non-finite values.
Results may differ from a plain program's by a relative error of at most 0.0056.
Values may be sent and summed in bfloat16 or wider, within the bound.
No kernel may reach another device: no remote copies, remote signals or barrier semaphores. Data moves between devices by JAX's collectives and lax.ppermute only.
A program may use at most 128 MiB of HBM per device.

v0:
```python
import jax
import jax.numpy as jnp
from jax import lax
from jax.sharding import PartitionSpec as P

SNPS = 500
FOLDS = 5


def standardize(genotype, allele_freq):
    spread = jnp.sqrt(2.0 * allele_freq * (1.0 - allele_freq))
    return ((genotype.astype(jnp.float32) - 2.0 * allele_freq) / spread).astype(jnp.bfloat16)


def solve_pair(factor, target):
    return jax.scipy.linalg.cho_solve((factor, True), target)


def predict(columns, weights):
    stacked = jnp.transpose(weights, (2, 0, 1)).reshape(-1, weights.shape[1])
    product = lax.dot_general(
        stacked, columns, (((1,), (1,)), ((), ())), preferred_element_type=jnp.float32
    )
    return product.astype(jnp.bfloat16).reshape(
        weights.shape[2], weights.shape[0], columns.shape[0]
    )


def inner_products(left_cols, right_cols):
    return lax.dot_general(
        left_cols, right_cols, (((0,), (0,)), ((), ())), preferred_element_type=jnp.float32
    )


def tile_pairs():
    pairs = []
    for row_tile in range(4):
        for col_tile in range(row_tile, 4):
            pairs.append((row_tile, col_tile))
    return pairs


def tile_grams(left_cols, right_cols, tile_width):
    tile_list = []
    for row_tile, col_tile in tile_pairs():
        first = left_cols[:, row_tile * tile_width : (row_tile + 1) * tile_width]
        second = right_cols[:, col_tile * tile_width : (col_tile + 1) * tile_width]
        tile_list.append(inner_products(first, second))
    return jnp.stack(tile_list)


def rebuild(tile_stack):
    pairs = tile_pairs()
    band_rows = []
    for row_tile in range(4):
        band_row = []
        for col_tile in range(4):
            if row_tile <= col_tile:
                band_row.append(tile_stack[pairs.index((row_tile, col_tile))])
            else:
                band_row.append(jnp.transpose(tile_stack[pairs.index((col_tile, row_tile))]))
        band_rows.append(jnp.concatenate(band_row, axis=1))
    return jnp.concatenate(band_rows, axis=0)


def shared_solve(rest_grams, rest_crosses, shrinkage, counts):
    member_count = rest_grams.shape[1]
    width = rest_grams.shape[-1]
    traits = rest_crosses.shape[-1]
    ridge_count = shrinkage.shape[0]
    systems = FOLDS * member_count * ridge_count
    devices = lax.axis_size("sample")
    share = -(-systems // devices)
    flat_grams = rest_grams.reshape(FOLDS * member_count, width, width)
    flat_crosses = rest_crosses.reshape(FOLDS * member_count, width, traits)
    flat_counts = jnp.repeat(counts, member_count)
    owned_ids = lax.axis_index("sample") * share + lax.broadcasted_iota(jnp.int32, (share,), 0)
    owned_ids = jnp.minimum(owned_ids, systems - 1)
    pair_ids = owned_ids // ridge_count
    ridge_ids = owned_ids % ridge_count
    chosen_counts = jnp.take(flat_counts, pair_ids, axis=0)
    system = jnp.take(flat_grams, pair_ids, axis=0) / chosen_counts[:, None, None]
    target = jnp.take(flat_crosses, pair_ids, axis=0) / chosen_counts[:, None, None]
    identity = jnp.eye(width, dtype=jnp.float32)
    full = system + jnp.take(shrinkage, ridge_ids, axis=0)[:, None, None] * identity
    factor = jnp.linalg.cholesky(full)
    solved = jax.vmap(solve_pair, (0, 0))(factor, target).astype(jnp.bfloat16)
    collected = lax.all_gather(solved, "sample", axis=0, tiled=True)
    return collected[:systems].reshape(FOLDS, member_count, ridge_count, width, traits)


def shards(genotype, allele_freq, phenotype, shrinkage, owner_order):
    sample_rows = genotype.shape[0]
    total_rows = sample_rows * lax.axis_size("sample")
    scaled = standardize(genotype, allele_freq)
    ordered = jnp.take(phenotype, owner_order, axis=1)
    local_blocks = allele_freq.shape[0] // SNPS
    tile_width = SNPS // 4
    column_sets = [scaled[:, member * SNPS : (member + 1) * SNPS] for member in range(local_blocks)]
    bounds = [-(-(k * total_rows) // FOLDS) for k in range(FOLDS + 1)]
    counts = jnp.array(
        [float(total_rows - (bounds[k + 1] - bounds[k])) for k in range(FOLDS)], dtype=jnp.float32
    )
    start_row = lax.axis_index("sample") * sample_rows
    row_ids = start_row + lax.broadcasted_iota(jnp.int32, (sample_rows,), 0)
    fold_of = row_ids * FOLDS // total_rows
    first_fold = start_row * FOLDS // total_rows
    slot_folds = [first_fold, first_fold + 1]
    slot_masks = [fold_of == slot_folds[0], fold_of == slot_folds[1]]
    picked = jnp.minimum(jnp.stack(slot_folds), FOLDS - 1)
    fold_ids = jnp.arange(FOLDS, dtype=jnp.int32)

    def fold_partials(member):
        columns = column_sets[member]
        gram_total = jnp.zeros((FOLDS, 10, tile_width, tile_width), jnp.float32)
        cross_total = jnp.zeros((FOLDS, SNPS, ordered.shape[1]), jnp.float32)
        for slot in range(2):
            masked = jnp.where(slot_masks[slot][:, None], columns, jnp.zeros_like(columns))
            selector = (fold_ids == slot_folds[slot]).astype(jnp.float32)
            gram_total = (
                gram_total
                + selector[:, None, None, None] * tile_grams(masked, columns, tile_width)[None]
            )
            cross_total = (
                cross_total + selector[:, None, None] * inner_products(masked, ordered)[None]
            )
        return (gram_total, cross_total)

    def weights_for(members):
        parts = [fold_partials(member) for member in members]
        grams = jnp.stack([item[0] for item in parts], axis=1)
        crosses = jnp.stack([item[1] for item in parts], axis=1)
        summed_grams, summed_crosses = lax.psum((grams, crosses), "sample")
        whole = jax.vmap(jax.vmap(rebuild))(summed_grams)
        rest_grams = jnp.sum(whole, axis=0)[None] - whole
        rest_crosses = jnp.sum(summed_crosses, axis=0)[None] - summed_crosses
        every_weights = shared_solve(rest_grams, rest_crosses, shrinkage, counts)
        return jnp.take(every_weights, picked, axis=0)

    def fold_predictions(member, slot_weights):
        columns = column_sets[member]
        lower = predict(columns, slot_weights[0])
        upper = predict(columns, slot_weights[1])
        return jnp.where(slot_masks[1][None, None, :], upper, lower)

    weights = weights_for(list(range(local_blocks)))
    local_preds = jnp.concatenate(
        [fold_predictions(member, weights[:, member]) for member in range(local_blocks)], axis=1
    )
    return lax.all_to_all(local_preds, "block", split_axis=0, concat_axis=1, tiled=True)


def solution(mesh):
    in_specs = (P("sample", "block"), P("block"), P("sample", None), P(), P())
    out_specs = P("block", None, "sample")
    return jax.shard_map(shards, mesh=mesh, in_specs=in_specs, out_specs=out_specs, check_vma=False)
```

profile of v0, /device:TPU:0, one launch (start us, length us, event | category | flops | bytes accessed | tf_op | source)
XLA Modules:
  0.0 596.3 jit_solution(1321422785324491491)
XLA Ops:
  8.6 2.7 divide_convert_fusion
  31.1 3.5 pad_maximum_fusion
  40.3 146.0 %all-reduce.6.cloned.1.call-done = (f32[5,2,10,125,125]{4,3,1,0,2:T(8,128)}, f32[5,2,500,16]{2,3,1,0:T(8,128)}) async-done(((f32[5,2,10,125,125]{4,3,1,0,2:T(8,128)}, f32[5,2,500,16]{2,3,1,0:T(8,128)}), (f32[5,2,10,125,125]{4,3,1,0,2:T(8,128)}, f32[5,2,500,16]{2,3,1,0:T(8,128)})) %all-reduce.6.cloned.1.call-update) | async-done | bytes 6570016 | tf_op jit(solution)/shard_map/psum | solution.py:133
  186.3 7.2 %slice_bitcast_fusion.19 = (f32[5,2,125,125]{3,2,1,0:T(8,128)}, f32[5,2,125,125]{3,2,1,0:T(8,128)}, f32[5,2,125,125]{2,3,1,0:T(8,128)}, f32[5,2,125,125]{3,2,1,0...) fusion(f32[5,2,10,125,125]{4,3,1,0,2:T(8,128)} %get-tuple-eleme, ...), kind=kLoop, calls=%fused_computation.355 | loop fusion | bytes 18125000 | tf_op jit(solution)/shard_map/vmap(vmap())/squeeze | solution.py:59
  193.5 2.2 slice.448
  197.1 2.2 copy.244
  200.9 2.2 copy.306
  203.1 2.2 copy.250
  205.3 2.2 copy.307
  207.5 3.1 pad_maximum_fusion.1
  210.6 3.3 copy.246
  214.0 12.1 %maximum_reduce_fusion = f32[2,500,500]{2,1,0:T(8,128)S(1)} fusion(f32[5,2,125,125]{3,2,1,0:T(8,128)} %get-tuple-element.37, f32[5,2,125,125]{3,2,1,0:T(8,128)} %copy.245, f32[5,2,125,125]{3,2,1,0:T(8,128)S(1)} %bitcast.329, f32[5,2,125,125]{3,2,1,0:T(8,128)} %copy.244, f32[5,2,125,125]{3,2,1,0:T(8,128)} %get-tuple-element.33, ...), kind=kLoop, calls=%fused_computation.8 | loop fusion | flops 32000000 | bytes 12000000 | tf_op jit(solution)/shard_map/reduce_sum | solution.py:135
  226.2 43.5 %maximum_subtract_fusion = f32[10,500,500]{2,1,0:T(8,128)} fusion(f32[10,125,125]{2,1,0:T(8,128)S(1)} %bitcast.345, f32[10,125,125]{2,1,0:T(8,128)S(1)} %bitcast.338, f32[10,125,125]{2,1,0:T(8,128)S(1)} %bitcast.330, f32[10,125,125]{2,1,0:T(8,128)S(1)} %bitcast.339, f32[10,125,125]{2,1,0:T(8,128)S(1)} %bitcast.344, f32[10,125,125]{2,1,0:T(8,128)S(1)} %bitcast.343, ...), kind=kLoop, calls=%fused_computation.9 | loop fusion | flops 40000000 | bytes 22000000 | tf_op jit(solution)/shard_map/sub | solution.py:135
  269.8 5.9 gather_fusion
  275.7 3.2 select_divide_fusion
  278.9 3.0 copy.256
  281.9 3.4 fusion.1
  286.7 23.7 %custom-call.38 = f32[2,128,128]{2,1,0:T(8,128)S(1)} custom-call(f32[2,128,128]{2,1,0:T(8,128)S(1)} %copy.257), custom_call_target="Cholesky" | custom-call | tf_op jit(solution)/shard_map/jit(cholesky)/cholesky | solution.py:86
  311.9 19.7 %custom-call.39 = f32[2,1,128,128]{2,3,1,0:T(8,128)S(1)} custom-call(f32[2,1,128,128]{3,2,1,0:T(8,128)S(1)} %select_bitcast_fusion.2), custom_call_target="InvertDiagBlocksLowerTriangular" | custom-call | tf_op jit(solution)/shard_map/jit(cholesky)/cholesky | solution.py:86
  331.6 2.6 constant_dynamic-update-slice_fusion.3
  335.9 23.5 %custom-call.40 = f32[2,128,128]{2,1,0:T(8,128)S(1)} custom-call(f32[2,128,128]{2,1,0:T(8,128)S(1)} %copy.262), custom_call_target="Cholesky" | custom-call | tf_op jit(solution)/shard_map/jit(cholesky)/cholesky | solution.py:86
  360.1 20.1 %custom-call.41 = f32[2,1,128,128]{2,3,1,0:T(8,128)S(1)} custom-call(f32[2,1,128,128]{3,2,1,0:T(8,128)S(1)} %get-tuple-element.59), custom_call_target="InvertDiagBlocksLowerTriangular" | custom-call | tf_op jit(solution)/shard_map/jit(cholesky)/cholesky | solution.py:86
  383.5 23.5 %custom-call.42 = f32[2,128,128]{2,1,0:T(8,128)S(1)} custom-call(f32[2,128,128]{2,1,0:T(8,128)S(1)} %copy.267), custom_call_target="Cholesky" | custom-call | tf_op jit(solution)/shard_map/jit(cholesky)/cholesky | solution.py:86
  407.7 19.7 %custom-call.43 = f32[2,1,128,128]{2,3,1,0:T(8,128)S(1)} custom-call(f32[2,1,128,128]{3,2,1,0:T(8,128)S(1)} %get-tuple-element.57), custom_call_target="InvertDiagBlocksLowerTriangular" | custom-call | tf_op jit(solution)/shard_map/jit(cholesky)/cholesky | solution.py:86
  430.2 21.5 %custom-call.44 = f32[2,116,116]{2,1,0:T(8,128)S(1)} custom-call(f32[2,116,116]{2,1,0:T(8,128)S(1)} %copy.271), custom_call_target="Cholesky" | custom-call | tf_op jit(solution)/shard_map/jit(cholesky)/cholesky | solution.py:86
  456.2 9.2 %while.1 = (s32[]{:T(128)}, f32[2,500,500]{2,1,0:T(8,128)}, s32[3,2]{0,1:T(2,128)S(1)}, f32[3,2,128,128]{3,2,0,1:T(8,128)S(1)}, s32[]{:T(128)}) while((s32[]{:T(128)}, f32[2,500,500]{2,1,0:T(8,128)}, s32[3,2]{0,1:T(2,128)S(1)}, f32[3,2,128,128]{3,2,0,1:T(8,128)S(1)}, s32[]{:T(128)}) %tuple.71), condition=%wide.while_cond, body=%wide.while_body.sunk | while | flops 2 | bytes 262261 | solution.py:16
  456.9 2.4 bitcast_dynamic-update-slice_fusion.2
  460.0 2.4 bitcast_dynamic-update-slice_fusion.2
  463.1 2.4 bitcast_dynamic-update-slice_fusion.2
  466.5 79.4 %custom-call.45 = f32[2,4,128,128]{2,3,1,0:T(8,128)S(1)} custom-call(f32[2,4,128,128]{3,2,1,0:T(8,128)} %pad_maximum_fusion.2), custom_call_target="InvertDiagBlocksLowerTriangular" | custom-call | tf_op jit(solution)/shard_map/vmap(jit(_cho_solve))/triangular_solve | solution.py:16
  556.7 21.9 %all_gather.3 = bf16[32,500,16]{1,2,0:T(8,128)(2,1)S(1)} all-gather(bf16[2,500,16]{1,2,0:T(8,128)(2,1)S(1)} %pad_maximum_fusion.5), channel_id=1, replica_groups=mesh['sample'=16,'block'=2] {'sample'}, dimensions={0}, use_global_device_ids=true | all-gather | bytes 544000 | tf_op jit(solution)/shard_map/all_gather | solution.py:88
  581.5 7.0 %all_to_all.18 = bf16[16,4,1024]{2,1,0:T(4,128)(2,1)S(1)} all-to-all(bf16[16,4,1024]{2,1,0:T(4,128)(2,1)S(1)} %pad_maximum_fusion.4), channel_id=1, replica_groups=mesh['sample'=16,'block'=2] {'block'}, dimensions={0} | all-to-all | bytes 262144 | tf_op jit(solution)/shard_map/all_to_all | solution.py:150
  (221 shorter events, 64.2 us)
Async XLA Ops:
  6.5 8.1 %copy-start = (bf16[1024,16]{0,1:T(8,128)(2,1)S(1)}, bf16[1024,16]{0,1:T(8,128)(2,1)}, u32[]{:S(2)}) copy-start(bf16[1024,16]{0,1:T(8,128)(2,1)} %param.8) | copy-start | bytes 98308
  6.5 179.8 %all-reduce.6.cloned.1.call-start = ((), (), s32[]{:S(2)}) async-start(), calls=%async_computation.1 | async-start | bytes 13762560 | tf_op jit(solution)/shard_map/psum | solution.py:133
  12.6 2.0 copy-start.15
  12.6 2.0 copy-start.17
  15.2 3.3 copy-start.14
  18.6 1.3 copy-start.18
  18.6 1.4 copy-start.29
  21.8 1.2 copy-start.16
  21.8 1.4 copy-start.28
  35.5 0.8 copy-start.2
  193.5 5.9 copy-start.7
  213.9 12.2 %copy-start.4 = (f32[5,2,1,125,125]{4,3,1,0,2:T(8,128)S(1)}, f32[5,2,1,125,125]{4,3,1,0,2:T(8,128)}, u32[]{:S(2)}) copy-start(f32[5,2,1,125,125]{4,3,1,0,2:T(8,128)} %get-tuple-element.38) | copy-start | bytes 1875004
  213.9 12.3 %copy-start.5 = (f32[5,2,1,125,125]{4,3,1,0,2:T(8,128)S(1)}, f32[5,2,1,125,125]{4,3,1,0,2:T(8,128)}, u32[]{:S(2)}) copy-start(f32[5,2,1,125,125]{4,3,1,0,2:T(8,128)} %get-tuple-element.39) | copy-start | bytes 1875004
  213.9 12.3 %copy-start.6 = (f32[5,2,1,125,125]{4,3,1,0,2:T(8,128)S(1)}, f32[5,2,1,125,125]{4,3,1,0,2:T(8,128)}, u32[]{:S(2)}) copy-start(f32[5,2,1,125,125]{4,3,1,0,2:T(8,128)} %get-tuple-element.40) | copy-start | bytes 1875004
  213.9 12.3 %copy-start.8 = (f32[5,2,1,125,125]{4,3,1,0,2:T(8,128)S(1)}, f32[5,2,1,125,125]{4,3,1,0,2:T(8,128)}, u32[]{:S(2)}) copy-start(f32[5,2,1,125,125]{4,3,1,0,2:T(8,128)} %copy-done.7) | copy-start | bytes 1875004
  213.9 12.3 %copy-start.9 = (f32[5,2,125,125]{3,2,1,0:T(8,128)S(1)}, f32[5,2,125,125]{3,2,1,0:T(8,128)}, u32[]{:S(2)}) copy-start(f32[5,2,125,125]{3,2,1,0:T(8,128)} %copy.245) | copy-start | bytes 1875004
  213.9 12.3 %copy-start.10 = (f32[5,2,125,125]{3,2,1,0:T(8,128)S(1)}, f32[5,2,125,125]{3,2,1,0:T(8,128)}, u32[]{:S(2)}) copy-start(f32[5,2,125,125]{3,2,1,0:T(8,128)} %copy.244) | copy-start | bytes 1875004
  213.9 12.3 %copy-start.11 = (f32[5,2,1,125,125]{3,4,1,0,2:T(8,128)S(1)}, f32[5,2,1,125,125]{3,4,1,0,2:T(8,128)}, u32[]{:S(2)}) copy-start(f32[5,2,1,125,125]{3,4,1,0,2:T(8,128)} %copy.306) | copy-start | bytes 1875004
  213.9 12.3 %copy-start.19 = (f32[5,2,1,125,125]{4,3,1,0,2:T(8,128)S(1)}, f32[5,2,1,125,125]{4,3,1,0,2:T(8,128)}, u32[]{:S(2)}) copy-start(f32[5,2,1,125,125]{4,3,1,0,2:T(8,128)} %get-tuple-element.41) | copy-start | bytes 1875004
  213.9 12.3 %copy-start.20 = (f32[5,2,1,125,125]{4,3,1,0,2:T(8,128)S(1)}, f32[5,2,1,125,125]{4,3,1,0,2:T(8,128)}, u32[]{:S(2)}) copy-start(f32[5,2,1,125,125]{4,3,1,0,2:T(8,128)} %get-tuple-element.42) | copy-start | bytes 1875004
  213.9 12.3 %copy-start.21 = (f32[5,2,1,125,125]{4,3,1,0,2:T(8,128)S(1)}, f32[5,2,1,125,125]{4,3,1,0,2:T(8,128)}, u32[]{:S(2)}) copy-start(f32[5,2,1,125,125]{4,3,1,0,2:T(8,128)} %get-tuple-element.43) | copy-start | bytes 1875004
  213.9 12.3 %copy-start.22 = (f32[5,2,1,125,125]{4,3,1,0,2:T(8,128)S(1)}, f32[5,2,1,125,125]{4,3,1,0,2:T(8,128)}, u32[]{:S(2)}) copy-start(f32[5,2,1,125,125]{4,3,1,0,2:T(8,128)} %get-tuple-element.44) | copy-start | bytes 1875004
  213.9 12.3 %copy-start.23 = (f32[5,2,1,125,125]{4,3,1,0,2:T(8,128)S(1)}, f32[5,2,1,125,125]{4,3,1,0,2:T(8,128)}, u32[]{:S(2)}) copy-start(f32[5,2,1,125,125]{4,3,1,0,2:T(8,128)} %get-tuple-element.46) | copy-start | bytes 1875004
  214.0 12.3 %copy-start.24 = (f32[5,2,1,125,125]{4,3,1,0,2:T(8,128)S(1)}, f32[5,2,1,125,125]{4,3,1,0,2:T(8,128)}, u32[]{:S(2)}) copy-start(f32[5,2,1,125,125]{4,3,1,0,2:T(8,128)} %slice.448) | copy-start | bytes 1875004
  214.0 12.3 %copy-start.25 = (f32[5,2,125,125]{3,2,1,0:T(8,128)S(1)}, f32[5,2,125,125]{3,2,1,0:T(8,128)}, u32[]{:S(2)}) copy-start(f32[5,2,125,125]{3,2,1,0:T(8,128)} %copy.250) | copy-start | bytes 1875004
  278.9 3.0 copy-start.13
  285.2 1.3 copy-start.12
  381.5 71.4 %copy-start.27 = (pred[500,500]{1,0:T(8,128)(4,1)S(1)}, pred[500,500]{1,0:T(8,128)(4,1)}, u32[]{:S(2)}) copy-start(pred[500,500]{1,0:T(8,128)(4,1)} %iota_compare_fusion.2) | copy-start | bytes 750004
  452.9 3.3 copy-start.30
  454.9 1.3 copy-start.3
  454.9 91.0 %copy-start.26 = (f32[5,2,500,16]{2,3,1,0:T(8,128)S(1)}, f32[5,2,500,16]{2,3,1,0:T(8,128)}, u32[]{:S(2)}) copy-start(f32[5,2,500,16]{2,3,1,0:T(8,128)} %get-tuple-element.25) | copy-start | bytes 960004
  580.7 8.5 %copy-start.1 = (bf16[1024,16]{0,1:T(8,128)(2,1)S(1)}, bf16[1024,16]{0,1:T(8,128)(2,1)}, u32[]{:S(2)}) copy-start(bf16[1024,16]{0,1:T(8,128)(2,1)} %param.8) | copy-start | bytes 98308
  (1 other events, 0.7 us)
Sparse Core Ops, SparseCore 0:
  35.7 150.5 all-reduce.5
where the time goes:
time: 606 us; the launch traced here: 596 us
  other arithmetic  316 us (52%)
  waiting for transfers between devices  146 us (24%)
  local copies, waits for them, and re-layouts  53.2 us (9%)
  matrix products  37.1 us (6%)
  blocking collectives  28.9 us (5%)
  between operations  14.6 us (2%)
    another operation x18, other arithmetic, shared_solve(): factor = jnp.linalg.cholesky(full)  154 us
    psum x1, waiting for transfers between devices, weights_for(): summed_grams, summed_crosses = lax.psum((grams, crosses), 'sample')  146 us
    another operation x9, other arithmetic, solve_pair(): return jax.scipy.linalg.cho_solve((factor, True), target)  83.2 us
    sub x1, other arithmetic, weights_for(): rest_grams = jnp.sum(whole, axis=0)[None] - whole  43.5 us
    all_gather x1, blocking collectives, shared_solve(): collected = lax.all_gather(solved, 'sample', axis=0, tiled=True)  21.9 us
    dot_general x44, matrix products, inner_products(): lax.dot_general(left_cols, right_cols, (((0,), (0,)), ((), ())), preferre...  15.5 us
    reduce_sum x1, other arithmetic, weights_for(): rest_grams = jnp.sum(whole, axis=0)[None] - whole  12.1 us
  transfers between devices with their start and end apart: 1, of which 1 were waited for; matrix products, arithmetic and copies ran while one was open for 1% of the time, Pallas kernels for 0%

commit v1 on v0

--- a/solution.py
+++ b/solution.py
@@ -1,3 +1,4 @@
+import functools
 import jax
 import jax.numpy as jnp
 from jax import lax
@@ -5,6 +6,22 @@
 
 SNPS = 500
 FOLDS = 5
+
+
+def trace_row(m, link_axis, along_dim):
+    n_all = lax.axis_size(link_axis)
+    pieces_in = [m]
+    for j in range(1, n_all):
+        pieces_in.append(
+            lax.ppermute(
+                pieces_in[j - 1], link_axis, [(ii, (ii - 1) % n_all) for ii in range(n_all)]
+            )
+        )
+    d_next = jnp.concatenate(pieces_in, axis=along_dim)
+    return jnp.roll(d_next, lax.axis_index(link_axis) * m.shape[along_dim], axis=along_dim)
+
+
+_drive_pipes = functools.partial(trace_row, link_axis="sample", along_dim=0)
 
 
 def standardize(genotype, allele_freq):
@@ -85,7 +102,7 @@
     full = system + jnp.take(shrinkage, ridge_ids, axis=0)[:, None, None] * identity
     factor = jnp.linalg.cholesky(full)
     solved = jax.vmap(solve_pair, (0, 0))(factor, target).astype(jnp.bfloat16)
-    collected = lax.all_gather(solved, "sample", axis=0, tiled=True)
+    collected = _drive_pipes(solved)
     return collected[:systems].reshape(FOLDS, member_count, ridge_count, width, traits)
 
 

time: 606 us -> 685 us (1.13)
  starting transfers between devices: 0.01 us -> 64.9 us
  blocking collectives: 28.9 us -> 7.01 us
  local copies, waits for them, and re-layouts: 53.2 us -> 72.3 us
  waiting for transfers between devices: 146 us -> 162 us
    ppermute x0 -> x15, starting transfers between devices: none -> 64.9 us  [trace_row(): lax.ppermute(pieces_in[j - 1], link_axis, [(ii, (ii - 1) % n_all) for ii...]
    all_gather x1 -> x0, blocking collectives: 21.9 us -> none  [shared_solve(): collected = lax.all_gather(solved, 'sample', axis=0, tiled=True)]
    unnamed x68 -> x97, local copies, waits for them, and re-layouts: 10.5 us -> 28.1 us
    ppermute x0 -> x15, waiting for transfers between devices: none -> 15.5 us  [trace_row(): lax.ppermute(pieces_in[j - 1], link_axis, [(ii, (ii - 1) % n_all) for ii...]
  transfers between devices with their start and end apart: 1 -> 16, of which waited for: 1 -> 16; matrix products, arithmetic and copies ran while one was open for 1% -> 2% of each run, Pallas kernels for 0% -> 0%
where the time goes in v1:
time: 685 us; the launch traced here: 675 us
  other arithmetic  317 us (46%)
  waiting for transfers between devices  162 us (24%)
  local copies, waits for them, and re-layouts  72.3 us (11%)
  starting transfers between devices  64.9 us (9%)
  matrix products  37.3 us (5%)
  between operations  14.6 us (2%)
  blocking collectives  7.01 us (1%)
    another operation x18, other arithmetic, shared_solve(): factor = jnp.linalg.cholesky(full)  154 us
    psum x1, waiting for transfers between devices, weights_for(): summed_grams, summed_crosses = lax.psum((grams, crosses), 'sample')  146 us
    another operation x9, other arithmetic, solve_pair(): return jax.scipy.linalg.cho_solve((factor, True), target)  83.8 us
    ppermute x15, starting transfers between devices, trace_row(): lax.ppermute(pieces_in[j - 1], link_axis, [(ii, (ii - 1) % n_all) for ii...  64.9 us
    sub x1, other arithmetic, weights_for(): rest_grams = jnp.sum(whole, axis=0)[None] - whole  43.5 us
    unnamed x97, local copies, waits for them, and re-layouts  28.1 us
    dot_general x44, matrix products, inner_products(): lax.dot_general(left_cols, right_cols, (((0,), (0,)), ((), ())), preferre...  15.6 us
    ppermute x15, waiting for transfers between devices, trace_row(): lax.ppermute(pieces_in[j - 1], link_axis, [(ii, (ii - 1) % n_all) for ii...  15.5 us
  transfers between devices with their start and end apart: 16, of which 16 were waited for; matrix products, arithmetic and copies ran while one was open for 2% of the time, Pallas kernels for 0%

profile of v1, /device:TPU:0, one launch (start us, length us, event | category | flops | bytes accessed | tf_op | source)
XLA Modules:
  0.0 675.2 jit_solution(2702401880353005571)
XLA Ops:
  31.2 3.5 pad_maximum_fusion
  40.3 146.1 %all-reduce.6.cloned.1.call-done = (f32[5,2,10,125,125]{4,3,1,0,2:T(8,128)}, f32[5,2,500,16]{2,3,1,0:T(8,128)}) async-done(((f32[5,2,10,125,125]{4,3,1,0,2:T(8,128)}, f32[5,2,500,16]{2,3,1,0:T(8,128)}), (f32[5,2,10,125,125]{4,3,1,0,2:T(8,128)}, f32[5,2,500,16]{2,3,1,0:T(8,128)})) %all-reduce.6.cloned.1.call-update) | async-done | bytes 6570016 | tf_op jit(solution)/shard_map/psum | solution.py:150
  186.4 7.2 %slice_bitcast_fusion.19 = (f32[5,2,125,125]{3,2,1,0:T(8,128)}, f32[5,2,125,125]{3,2,1,0:T(8,128)}, f32[5,2,125,125]{2,3,1,0:T(8,128)}, f32[5,2,125,125]{3,2,1,0...) fusion(f32[5,2,10,125,125]{4,3,1,0,2:T(8,128)} %get-tuple-eleme, ...), kind=kLoop, calls=%fused_computation.388 | loop fusion | bytes 18125000 | tf_op jit(solution)/shard_map/vmap(vmap())/squeeze | solution.py:76
  210.7 3.2 copy.196
  214.0 12.1 %maximum_reduce_fusion = f32[2,500,500]{2,1,0:T(8,128)S(1)} fusion(f32[5,2,125,125]{3,2,1,0:T(8,128)} %get-tuple-element.37, f32[5,2,125,125]{3,2,1,0:T(8,128)} %copy.195, f32[5,2,125,125]{3,2,1,0:T(8,128)S(1)} %bitcast.329, f32[5,2,125,125]{3,2,1,0:T(8,128)} %copy.194, f32[5,2,125,125]{3,2,1,0:T(8,128)} %get-tuple-element.33, ...), kind=kLoop, calls=%fused_computation.8 | loop fusion | flops 32000000 | bytes 12000000 | tf_op jit(solution)/shard_map/reduce_sum | solution.py:152
  226.3 43.5 %maximum_subtract_fusion = f32[10,500,500]{2,1,0:T(8,128)} fusion(f32[10,125,125]{2,1,0:T(8,128)S(1)} %bitcast.345, f32[10,125,125]{2,1,0:T(8,128)S(1)} %bitcast.338, f32[10,125,125]{2,1,0:T(8,128)S(1)} %bitcast.330, f32[10,125,125]{2,1,0:T(8,128)S(1)} %bitcast.339, f32[10,125,125]{2,1,0:T(8,128)S(1)} %bitcast.344, f32[10,125,125]{2,1,0:T(8,128)S(1)} %bitcast.343, ...), kind=kLoop, calls=%fused_computation.9 | loop fusion | flops 40000000 | bytes 22000000 | tf_op jit(solution)/shard_map/sub | solution.py:152
  269.8 6.0 gather_fusion
  282.0 3.4 fusion.1
  286.8 23.7 %custom-call.38 = f32[2,128,128]{2,1,0:T(8,128)S(1)} custom-call(f32[2,128,128]{2,1,0:T(8,128)S(1)} %copy.207), custom_call_target="Cholesky" | custom-call | tf_op jit(solution)/shard_map/jit(cholesky)/cholesky | solution.py:103
  312.0 19.7 %custom-call.39 = f32[2,1,128,128]{2,3,1,0:T(8,128)S(1)} custom-call(f32[2,1,128,128]{3,2,1,0:T(8,128)S(1)} %select_bitcast_fusion.2), custom_call_target="InvertDiagBlocksLowerTriangular" | custom-call | tf_op jit(solution)/shard_map/jit(cholesky)/cholesky | solution.py:103
  336.1 23.5 %custom-call.40 = f32[2,128,128]{2,1,0:T(8,128)S(1)} custom-call(f32[2,128,128]{2,1,0:T(8,128)S(1)} %copy.212), custom_call_target="Cholesky" | custom-call | tf_op jit(solution)/shard_map/jit(cholesky)/cholesky | solution.py:103
  360.2 20.1 %custom-call.41 = f32[2,1,128,128]{2,3,1,0:T(8,128)S(1)} custom-call(f32[2,1,128,128]{3,2,1,0:T(8,128)S(1)} %get-tuple-element.59), custom_call_target="InvertDiagBlocksLowerTriangular" | custom-call | tf_op jit(solution)/shard_map/jit(cholesky)/cholesky | solution.py:103
  383.7 23.5 %custom-call.42 = f32[2,128,128]{2,1,0:T(8,128)S(1)} custom-call(f32[2,128,128]{2,1,0:T(8,128)S(1)} %copy.217), custom_call_target="Cholesky" | custom-call | tf_op jit(solution)/shard_map/jit(cholesky)/cholesky | solution.py:103
  407.9 19.7 %custom-call.43 = f32[2,1,128,128]{2,3,1,0:T(8,128)S(1)} custom-call(f32[2,1,128,128]{3,2,1,0:T(8,128)S(1)} %get-tuple-element.57), custom_call_target="InvertDiagBlocksLowerTriangular" | custom-call | tf_op jit(solution)/shard_map/jit(cholesky)/cholesky | solution.py:103
  430.5 21.5 %custom-call.44 = f32[2,116,116]{2,1,0:T(8,128)S(1)} custom-call(f32[2,116,116]{2,1,0:T(8,128)S(1)} %copy.221), custom_call_target="Cholesky" | custom-call | tf_op jit(solution)/shard_map/jit(cholesky)/cholesky | solution.py:103
  456.5 9.1 %while.1 = (s32[]{:T(128)}, f32[2,500,500]{2,1,0:T(8,128)}, s32[3,2]{0,1:T(2,128)S(1)}, f32[3,2,128,128]{3,2,0,1:T(8,128)S(1)}, s32[]{:T(128)}) while((s32[]{:T(128)}, f32[2,500,500]{2,1,0:T(8,128)}, s32[3,2]{0,1:T(2,128)S(1)}, f32[3,2,128,128]{3,2,0,1:T(8,128)S(1)}, s32[]{:T(128)}) %tuple.73), condition=%wide.while_cond, body=%wide.while_body.sunk | while | flops 2 | bytes 262261 | solution.py:33
  466.6 79.4 %custom-call.45 = f32[2,4,128,128]{2,3,1,0:T(8,128)S(1)} custom-call(f32[2,4,128,128]{3,2,1,0:T(8,128)} %pad_maximum_fusion.2), custom_call_target="InvertDiagBlocksLowerTriangular" | custom-call | tf_op jit(solution)/shard_map/vmap(jit(_cho_solve))/triangular_solve | solution.py:33
  561.7 4.4 collective-permute-start.1
  567.7 4.4 collective-permute-start.2
  573.8 4.4 collective-permute-start.3
  579.8 4.4 collective-permute-start.4
  585.9 4.4 collective-permute-start.5
  591.9 4.4 collective-permute-start.6
  597.9 4.4 collective-permute-start.7
  604.0 4.4 collective-permute-start.8
  610.0 4.4 collective-permute-start.9
  616.0 4.4 collective-permute-start.10
  622.1 4.4 collective-permute-start.11
  628.1 4.4 collective-permute-start.12
  634.1 4.4 collective-permute-start.13
  640.2 4.4 collective-permute-start.14
  660.4 7.0 %all_to_all.18 = bf16[16,4,1024]{2,1,0:T(4,128)(2,1)S(1)} all-to-all(bf16[16,4,1024]{2,1,0:T(4,128)(2,1)S(1)} %pad_maximum_fusion.4), channel_id=1, replica_groups=mesh['sample'=16,'block'=2] {'block'}, dimensions={0} | all-to-all | bytes 262144 | tf_op jit(solution)/shard_map/all_to_all | solution.py:167
  (280 shorter events, 135.5 us)
Async XLA Ops:
  6.5 179.8 %all-reduce.6.cloned.1.call-start = ((), (), s32[]{:S(2)}) async-start(), calls=%async_computation.1 | async-start | bytes 13762560 | tf_op jit(solution)/shard_map/psum | solution.py:150
  213.9 12.2 %copy-start.4 = (f32[5,2,1,125,125]{4,3,1,0,2:T(8,128)S(1)}, f32[5,2,1,125,125]{4,3,1,0,2:T(8,128)}, u32[]{:S(2)}) copy-start(f32[5,2,1,125,125]{4,3,1,0,2:T(8,128)} %get-tuple-element.38) | copy-start | bytes 1875004
  213.9 12.3 %copy-start.5 = (f32[5,2,1,125,125]{4,3,1,0,2:T(8,128)S(1)}, f32[5,2,1,125,125]{4,3,1,0,2:T(8,128)}, u32[]{:S(2)}) copy-start(f32[5,2,1,125,125]{4,3,1,0,2:T(8,128)} %get-tuple-element.39) | copy-start | bytes 1875004
  213.9 12.3 %copy-start.6 = (f32[5,2,1,125,125]{4,3,1,0,2:T(8,128)S(1)}, f32[5,2,1,125,125]{4,3,1,0,2:T(8,128)}, u32[]{:S(2)}) copy-start(f32[5,2,1,125,125]{4,3,1,0,2:T(8,128)} %get-tuple-element.40) | copy-start | bytes 1875004
  213.9 12.3 %copy-start.8 = (f32[5,2,1,125,125]{4,3,1,0,2:T(8,128)S(1)}, f32[5,2,1,125,125]{4,3,1,0,2:T(8,128)}, u32[]{:S(2)}) copy-start(f32[5,2,1,125,125]{4,3,1,0,2:T(8,128)} %copy-done.7) | copy-start | bytes 1875004
  213.9 12.3 %copy-start.9 = (f32[5,2,125,125]{3,2,1,0:T(8,128)S(1)}, f32[5,2,125,125]{3,2,1,0:T(8,128)}, u32[]{:S(2)}) copy-start(f32[5,2,125,125]{3,2,1,0:T(8,128)} %copy.195) | copy-start | bytes 1875004
  213.9 12.3 %copy-start.10 = (f32[5,2,125,125]{3,2,1,0:T(8,128)S(1)}, f32[5,2,125,125]{3,2,1,0:T(8,128)}, u32[]{:S(2)}) copy-start(f32[5,2,125,125]{3,2,1,0:T(8,128)} %copy.194) | copy-start | bytes 1875004
  213.9 12.3 %copy-start.11 = (f32[5,2,1,125,125]{3,4,1,0,2:T(8,128)S(1)}, f32[5,2,1,125,125]{3,4,1,0,2:T(8,128)}, u32[]{:S(2)}) copy-start(f32[5,2,1,125,125]{3,4,1,0,2:T(8,128)} %copy.256) | copy-start | bytes 1875004
  214.0 12.3 %copy-start.19 = (f32[5,2,1,125,125]{4,3,1,0,2:T(8,128)S(1)}, f32[5,2,1,125,125]{4,3,1,0,2:T(8,128)}, u32[]{:S(2)}) copy-start(f32[5,2,1,125,125]{4,3,1,0,2:T(8,128)} %get-tuple-element.41) | copy-start | bytes 1875004
  214.0 12.3 %copy-start.20 = (f32[5,2,1,125,125]{4,3,1,0,2:T(8,128)S(1)}, f32[5,2,1,125,125]{4,3,1,0,2:T(8,128)}, u32[]{:S(2)}) copy-start(f32[5,2,1,125,125]{4,3,1,0,2:T(8,128)} %get-tuple-element.42) | copy-start | bytes 1875004
  214.0 12.3 %copy-start.21 = (f32[5,2,1,125,125]{4,3,1,0,2:T(8,128)S(1)}, f32[5,2,1,125,125]{4,3,1,0,2:T(8,128)}, u32[]{:S(2)}) copy-start(f32[5,2,1,125,125]{4,3,1,0,2:T(8,128)} %get-tuple-element.43) | copy-start | bytes 1875004
  214.0 12.3 %copy-start.22 = (f32[5,2,1,125,125]{4,3,1,0,2:T(8,128)S(1)}, f32[5,2,1,125,125]{4,3,1,0,2:T(8,128)}, u32[]{:S(2)}) copy-start(f32[5,2,1,125,125]{4,3,1,0,2:T(8,128)} %get-tuple-element.44) | copy-start | bytes 1875004
  214.0 12.3 %copy-start.23 = (f32[5,2,1,125,125]{4,3,1,0,2:T(8,128)S(1)}, f32[5,2,1,125,125]{4,3,1,0,2:T(8,128)}, u32[]{:S(2)}) copy-start(f32[5,2,1,125,125]{4,3,1,0,2:T(8,128)} %get-tuple-element.46) | copy-start | bytes 1875004
  214.0 12.3 %copy-start.24 = (f32[5,2,1,125,125]{4,3,1,0,2:T(8,128)S(1)}, f32[5,2,1,125,125]{4,3,1,0,2:T(8,128)}, u32[]{:S(2)}) copy-start(f32[5,2,1,125,125]{4,3,1,0,2:T(8,128)} %slice.448) | copy-start | bytes 1875004
  214.0 12.3 %copy-start.25 = (f32[5,2,125,125]{3,2,1,0:T(8,128)S(1)}, f32[5,2,125,125]{3,2,1,0:T(8,128)}, u32[]{:S(2)}) copy-start(f32[5,2,125,125]{3,2,1,0:T(8,128)} %copy.200) | copy-start | bytes 1875004
  381.6 71.5 %copy-start.27 = (pred[500,500]{1,0:T(8,128)(4,1)S(1)}, pred[500,500]{1,0:T(8,128)(4,1)}, u32[]{:S(2)}) copy-start(pred[500,500]{1,0:T(8,128)(4,1)} %iota_compare_fusion.2) | copy-start | bytes 750004
  455.2 90.8 %copy-start.26 = (f32[5,2,500,16]{2,3,1,0:T(8,128)S(1)}, f32[5,2,500,16]{2,3,1,0:T(8,128)}, u32[]{:S(2)}) copy-start(f32[5,2,500,16]{2,3,1,0:T(8,128)} %get-tuple-element.25) | copy-start | bytes 960004
  557.4 4.3 collective-permute-start
  561.7 6.0 collective-permute-start.1
  567.7 6.0 collective-permute-start.2
  573.8 6.0 collective-permute-start.3
  579.8 6.0 collective-permute-start.4
  585.9 6.0 collective-permute-start.5
  591.9 6.0 collective-permute-start.6
  597.9 6.0 collective-permute-start.7
  604.0 6.0 collective-permute-start.8
  610.0 6.0 collective-permute-start.9
  616.0 6.0 collective-permute-start.10
  622.1 6.0 collective-permute-start.11
  628.1 6.0 collective-permute-start.12
  634.1 6.0 collective-permute-start.13
  640.2 6.0 collective-permute-start.14
  (16 other events, 46.0 us)
Sparse Core Ops, SparseCore 0:
  35.8 150.5 all-reduce.5
